TPU v7x, 128 devices: a whole 4x4x4 slice. The times are simulated.
128 devices in a mesh: dp: 16 (over x, z_lo, core), ctx: 8 (over z_hi, y).
Axes of the slice: x: 4, y: 4, z: 4 (z_hi: 2, z_lo: 2; z = z_hi * 2 + z_lo), core: 2. Of those that a mesh axis runs over, the one named last changes fastest.
Arguments:
- query_rows: bfloat16 [16, 2048, 2048], P('dp', 'ctx'), may hold values from -6 to 6
- key_rows: bfloat16 [16, 2048, 2048], P('dp', 'ctx'), may hold values from -6 to 6
- value_rows: bfloat16 [16, 2048, 2048], P('dp', 'ctx'), may hold values from -6 to 6
- utt_lengths: int32 [16, 8], P('dp'), may hold values from 1 to 1024, 2048 in all within a row
- out_weight: bfloat16 [2048, 4096], P('dp'), may hold values from -0.5 to 0.5
Outputs:
- out_rows: bfloat16 [16, 2048, 4096], P('dp', 'ctx')
Inputs may be any that keep to these rules, and one draw needn't show every extreme that they name: `utt_lengths`: the 8 lengths of each sequence sum to 2048, and in each sequence one utterance has exactly 1024 frames.
All inputs are finite; a program needn't handle non-finite values.
Results may differ from a plain program's by a relative error of at most 0.015.
Values may be sent and summed in bfloat16 or wider, within the bound.
No kernel may reach another device: no remote copies, remote signals or barrier semaphores. Data moves between devices by JAX's collectives and lax.ppermute only.
A program may use at most 192 MiB of HBM per device.

v0:
```python
import jax
import jax.numpy as jnp
from jax import lax
from jax.sharding import PartitionSpec as P

HQ = 16
HD = 128


big_negative = -1e30


def segment_ids(utt_ends, first_frame, frames):
    positions = first_frame + jnp.arange(frames, dtype=jnp.int32)
    return jnp.sum((positions[:, None] >= utt_ends[None, :]).astype(jnp.int32), axis=1)


def attend(carry_state, query_heads, query_seg, kv_block, key_seg):
    frames = kv_block.shape[1]
    key_heads = kv_block[0].reshape(frames, -1, HD)
    value_heads = kv_block[1].reshape(frames, -1, HD)
    allowed = (query_seg[:, None] == key_seg[None, :])[:, None, :]
    scores = jnp.einsum(
        "qhd,khd->qhk", query_heads, key_heads, preferred_element_type=jnp.float32
    ) * HD ** (-0.5)
    masked = jnp.where(allowed, scores, big_negative)
    block_max = jnp.max(masked, axis=2)
    max_new = block_max if carry_state is None else jnp.maximum(carry_state[0], block_max)
    weights = jnp.exp(masked - max_new[:, :, None])
    denom_new = jnp.sum(weights, axis=2)
    numerator = jnp.einsum(
        "qhk,khd->qhd",
        weights.astype(jnp.bfloat16),
        value_heads,
        preferred_element_type=jnp.float32,
    )
    if carry_state is not None:
        max_old, denom_old, numerator_old = carry_state
        rescale = jnp.exp(max_old - max_new)
        denom_new = denom_old * rescale + denom_new
        numerator = numerator_old * rescale[:, :, None] + numerator
    return (max_new, denom_new, numerator)


def shards(query_rows, key_rows, value_rows, utt_lengths, out_weight):
    frames = query_rows.shape[1]
    cycle_size = lax.axis_size("ctx")
    cycle_place = lax.axis_index("ctx")
    utt_ends = jnp.cumsum(utt_lengths[0])
    query_heads = query_rows[0].reshape(frames, HQ, HD)
    query_seg = segment_ids(utt_ends, cycle_place * frames, frames)

    def absorb(carry_state, kv_block, source, heads=slice(None)):
        key_seg = segment_ids(utt_ends, source * frames, frames)
        return attend(carry_state, query_heads[:, heads], query_seg, kv_block, key_seg)

    gathered_weight = lax.all_gather(out_weight, "dp", axis=0, tiled=True)
    kv_block = jnp.concatenate([key_rows, value_rows], axis=0)
    plane_size = cycle_size // 2
    plane = cycle_place // plane_size
    spot = cycle_place % plane_size
    half = frames // 2

    def in_plane(block, step):
        route = [
            (i, (i // plane_size) * plane_size + (i % plane_size + step) % plane_size)
            for i in range(cycle_size)
        ]
        return lax.ppermute(block, "ctx", route)

    def around(block, source_plane):
        ahead = in_plane(block, 1)
        behind = in_plane(block, -1)
        ahead_two = in_plane(ahead[:, :half], 1)
        behind_two = in_plane(behind[:, half:], -1)
        far = jnp.concatenate([ahead_two, behind_two], axis=1)
        base = source_plane * plane_size
        return [
            (ahead, base + (spot - 1) % plane_size),
            (behind, base + (spot + 1) % plane_size),
            (far, base + (spot + 2) % plane_size),
        ]

    partner = lax.ppermute(
        kv_block, "ctx", [(i, (i + plane_size) % cycle_size) for i in range(cycle_size)]
    )
    arrivals = [(kv_block, cycle_place)] + around(kv_block, plane)
    arrivals += [(partner, (cycle_place + plane_size) % cycle_size)]
    partner_ahead = in_plane(partner, 1)
    partner_behind = in_plane(partner, -1)
    arrivals += [
        (partner_ahead, (1 - plane) * plane_size + (spot - 1) % plane_size),
        (partner_behind, (1 - plane) * plane_size + (spot + 1) % plane_size),
    ]
    carry_state = None
    for block, source in arrivals:
        carry_state = lax.optimization_barrier(absorb(carry_state, block, source))
    far_source = (1 - plane) * plane_size + (spot + 2) % plane_size
    groups = 2
    width = HQ // groups
    pieces = []
    for group in range(groups):
        cols = slice(group * width * HD, (group + 1) * width * HD)
        pieces.append(
            (
                in_plane(partner_ahead[:, :half, cols], 1),
                in_plane(partner_behind[:, half:, cols], -1),
            )
        )
    summed = None
    for group in range(groups):
        heads = slice(group * width, (group + 1) * width)
        cols = slice(group * width * HD, (group + 1) * width * HD)
        if summed is not None:
            summed, pieces[group] = lax.optimization_barrier((summed, pieces[group]))
        far = jnp.concatenate(pieces[group], axis=1)
        group_state = tuple(part[:, heads] for part in carry_state)
        max_final, denom_final, numerator = absorb(group_state, far, far_source, heads)
        attn_rows = (numerator / denom_final[:, :, None]).reshape(frames, width * HD)
        partial = jnp.dot(
            attn_rows.astype(jnp.bfloat16),
            gathered_weight[cols],
            preferred_element_type=jnp.float32,
        )
        summed = partial if summed is None else summed + partial
    return summed.astype(jnp.bfloat16)[None]


def solution(mesh):
    return jax.shard_map(
        shards,
        mesh=mesh,
        in_specs=(
            P("dp", "ctx", None),
            P("dp", "ctx", None),
            P("dp", "ctx", None),
            P("dp", None),
            P("dp", None),
        ),
        out_specs=P("dp", "ctx", None),
        check_vma=False,
    )
```

profile of v0, /device:TPU:102, one launch (start us, length us, event | category | flops | bytes accessed | tf_op | source)
XLA Modules:
  0.0 195.1 jit_solution(7340920564767697299)
XLA Ops:
  7.3 1.5 copy.80
  8.8 1.5 copy.79
  10.2 1.5 pad_maximum_fusion
  11.7 1.6 collective-permute-start
  13.9 1.7 collective-permute-start.1
  15.5 1.5 copy.74
  17.2 1.4 copy.149
  18.7 1.6 copy.150
  21.8 1.4 fusion.72
  24.2 36.5 %collective-permute-done = bf16[2,256,2048]{1,2,0:T(8,128)(2,1)} collective-permute-done((bf16[2,256,2048]{1,2,0:T(8,128)(2,1)}, bf16[2,256,2048]{1,2,0:T(8,128)(2,1)}, u32[]{:S(2)}, u32[]{:S(2)}) %collective-permute-start) | collective-permute-done | bytes 2097184 | tf_op jit(solution)/shard_map/ppermute | solution.py:69
  60.7 1.7 fusion.123
  64.3 1.5 bitcast_add_fusion.5
  65.8 1.3 slice.132
  69.6 1.5 bitcast_add_fusion.4
  71.2 3.1 %collective-permute-start.3 = (bf16[2,128,2048]{1,2,0:T(8,128)(2,1)S(1)}, bf16[2,128,2048]{1,2,0:T(8,128)(2,1)S(1)}, u32[]{:S(2)}, u32[]{:S(2)}) collective-permute-start(bf16[2,128,2048]{1,2,0:T(8,128)(2,1)S(1)} %slice.133), channel_id=1, source_target_pairs={{0,3},{1,0},{2,1},{3,2},{4,7},{5,4},{6,5},{7,6},{8,11},{9,8},{10,9... | collective-permute-start | bytes 3145736 | tf_op jit(solution)/shard_map/ppermute | solution.py:69
  74.3 30.3 %collective-permute-done.4 = bf16[2,256,2048]{1,2,0:T(8,128)(2,1)} collective-permute-done((bf16[2,256,2048]{1,2,0:T(8,128)(2,1)}, bf16[2,256,2048]{1,2,0:T(8,128)(2,1)}, u32[]{:S(2)}, u32[]{:S(2)}) %collective-permute-start.4) | collective-permute-done | bytes 2097184 | tf_op jit(solution)/shard_map/ppermute | solution.py:84
  104.6 1.7 collective-permute-start.5
  106.3 1.6 collective-permute-start.6
  107.8 1.7 fusion.120
  113.0 1.5 bitcast_add_fusion.3
  115.4 1.5 bitcast_add_fusion.2
  117.0 32.7 %collective-permute-done.5 = bf16[2,256,2048]{1,2,0:T(8,128)(2,1)S(1)} collective-permute-done((bf16[2,256,2048]{1,2,0:T(8,128)(2,1)}, bf16[2,256,2048]{1,2,0:T(8,128)(2,1)S(1)}, u32[]{:S(2)}, u32[]{:S(2)}) %collective-permute-start.5) | collective-permute-done | bytes 2097184 | tf_op jit(solution)/shard_map/ppermute | solution.py:69
  150.6 1.7 collective-permute-start.7
  153.3 1.6 collective-permute-start.8
  156.8 1.5 bitcast_add_fusion.1
  160.4 1.5 bitcast_add_fusion
  162.5 2.8 %collective-permute-start.10 = (bf16[2,128,1024]{1,2,0:T(8,128)(2,1)}, bf16[2,128,1024]{1,2,0:T(8,128)(2,1)}, u32[]{:S(2)}, u32[]{:S(2)}) collective-permute-start(bf16[2,128,1024]{1,2,0:T(8,128)(2,1)} %get-tuple-element.77), channel_id=1, source_target_pairs={{0,3},{1,0},{2,1},{3,2},{4,7},{5,4},{6,5},{7,6},{8,11},{9,8},{10,9... | collective-permute-start | bytes 1572872 | tf_op jit(solution)/shard_map/ppermute | solution.py:69
  168.0 7.7 %fusion.2 = f32[256,4096]{1,0:T(8,128)} fusion(bf16[256,1024]{0,1:T(8,128)(2,1)S(1)} %bitcast.192, bf16[2048,4096]{1,0:T(8,128)(2,1)} %all-gather.2.cloned.1.call-done), kind=kOutput, calls=%fused_computation.2 | convolution fusion | flops 2147483648 | bytes 13107200 | tf_op jit(solution)/shard_map/dot_general | solution.py:120
  175.7 1.1 constant_dynamic-update-slice_fusion.5
  176.8 1.3 constant_dynamic-update-slice_fusion.4
  180.4 6.0 %fusion = f32[256,4096]{1,0:T(8,128)S(1)} fusion(bf16[256,1024]{0,1:T(8,128)(2,1)S(1)} %bitcast.193, bf16[2048,4096]{1,0:T(8,128)(2,1)} %all-gather.2.cloned.1.call-done), kind=kOutput, calls=%fused_computation | convolution fusion | flops 2147483648 | bytes 13107200 | tf_op jit(solution)/shard_map/dot_general | solution.py:120
  186.5 1.8 fusion.39
  (80 shorter events, 23.7 us)
Async XLA Ops:
  6.5 161.4 %all-gather.2.cloned.1.call-start = ((), (), s32[]{:S(2)}) async-start(), calls=%async_computation | async-start | bytes 17825792 | tf_op jit(solution)/shard_map/all_gather | solution.py:57
  8.7 8.3 %copy-start.3 = (s32[1,8]{1,0:T(1,128)S(1)}, s32[1,8]{1,0:T(1,128)}, u32[]{:S(2)}) copy-start(s32[1,8]{1,0:T(1,128)} %param.8) | copy-start | bytes 100
  11.7 49.0 %collective-permute-start = (bf16[2,256,2048]{1,2,0:T(8,128)(2,1)}, bf16[2,256,2048]{1,2,0:T(8,128)(2,1)}, u32[]{:S(2)}, u32[]{:S(2)}) collective-permute-start(bf16[2,256,2048]{1,2,0:T(8,128)(2,1)} %pad_maximum_fusion), channel_id=1, source_target_pairs={{0,1},{1,2},{2,3},{3,0},{4,5},{5,6},{6,7},{7,4},{8,9},{9,10},{10,1... | collective-permute-start | bytes 6291464 | tf_op jit(solution)/shard_map/ppermute | solution.py:69
  13.3 91.3 %collective-permute-start.4 = (bf16[2,256,2048]{1,2,0:T(8,128)(2,1)}, bf16[2,256,2048]{1,2,0:T(8,128)(2,1)}, u32[]{:S(2)}, u32[]{:S(2)}) collective-permute-start(bf16[2,256,2048]{1,2,0:T(8,128)(2,1)} %pad_maximum_fusion), channel_id=1, source_target_pairs={{0,4},{1,5},{2,6},{3,7},{4,0},{5,1},{6,2},{7,3},{8,12},{9,13},{10,... | collective-permute-start | bytes 6291464 | tf_op jit(solution)/shard_map/ppermute | solution.py:84
  13.9 53.8 %collective-permute-start.1 = (bf16[2,256,2048]{1,2,0:T(8,128)(2,1)}, bf16[2,256,2048]{1,2,0:T(8,128)(2,1)S(1)}, u32[]{:S(2)}, u32[]{:S(2)}) collective-permute-start(bf16[2,256,2048]{1,2,0:T(8,128)(2,1)} %pad_maximum_fusion), channel_id=1, source_target_pairs={{0,3},{1,0},{2,1},{3,2},{4,7},{5,4},{6,5},{7,6},{8,11},{9,8},{10,9... | collective-permute-start | bytes 6291464 | tf_op jit(solution)/shard_map/ppermute | solution.py:69
  67.1 43.4 %collective-permute-start.2 = (bf16[2,128,2048]{1,2,0:T(8,128)(2,1)S(1)}, bf16[2,128,2048]{1,2,0:T(8,128)(2,1)S(1)}, u32[]{:S(2)}, u32[]{:S(2)}) collective-permute-start(bf16[2,128,2048]{1,2,0:T(8,128)(2,1)S(1)} %slice.132), channel_id=1, source_target_pairs={{0,1},{1,2},{2,3},{3,0},{4,5},{5,6},{6,7},{7,4},{8,9},{9,10},{10,1... | collective-permute-start | bytes 3145736 | tf_op jit(solution)/shard_map/ppermute | solution.py:69
  71.2 39.5 %collective-permute-start.3 = (bf16[2,128,2048]{1,2,0:T(8,128)(2,1)S(1)}, bf16[2,128,2048]{1,2,0:T(8,128)(2,1)S(1)}, u32[]{:S(2)}, u32[]{:S(2)}) collective-permute-start(bf16[2,128,2048]{1,2,0:T(8,128)(2,1)S(1)} %slice.133), channel_id=1, source_target_pairs={{0,3},{1,0},{2,1},{3,2},{4,7},{5,4},{6,5},{7,6},{8,11},{9,8},{10,9... | collective-permute-start | bytes 3145736 | tf_op jit(solution)/shard_map/ppermute | solution.py:69
  104.6 45.0 %collective-permute-start.5 = (bf16[2,256,2048]{1,2,0:T(8,128)(2,1)}, bf16[2,256,2048]{1,2,0:T(8,128)(2,1)S(1)}, u32[]{:S(2)}, u32[]{:S(2)}) collective-permute-start(bf16[2,256,2048]{1,2,0:T(8,128)(2,1)} %collective-permute-done.4), channel_id=1, source_target_pairs={{0,1},{1,2},{2,3},{3,0},{4,5},{5,6},{6,7},{7,4},{8,9},{9,10},{10,1... | collective-permute-start | bytes 6291464 | tf_op jit(solution)/shard_map/ppermute | solution.py:69
  106.3 46.0 %collective-permute-start.6 = (bf16[2,256,2048]{1,2,0:T(8,128)(2,1)}, bf16[2,256,2048]{1,2,0:T(8,128)(2,1)S(1)}, u32[]{:S(2)}, u32[]{:S(2)}) collective-permute-start(bf16[2,256,2048]{1,2,0:T(8,128)(2,1)} %collective-permute-done.4), channel_id=1, source_target_pairs={{0,3},{1,0},{2,1},{3,2},{4,7},{5,4},{6,5},{7,6},{8,11},{9,8},{10,9... | collective-permute-start | bytes 6291464 | tf_op jit(solution)/shard_map/ppermute | solution.py:69
  150.6 14.6 %collective-permute-start.7 = (bf16[2,128,1024]{1,2,0:T(8,128)(2,1)S(1)}, bf16[2,128,1024]{1,2,0:T(8,128)(2,1)S(1)}, u32[]{:S(2)}, u32[]{:S(2)}) collective-permute-start(bf16[2,128,1024]{1,2,0:T(8,128)(2,1)S(1)} %get-tuple-element.80), channel_id=1, source_target_pairs={{0,1},{1,2},{2,3},{3,0},{4,5},{5,6},{6,7},{7,4},{8,9},{9,10},{10,1... | collective-permute-start | bytes 1572872 | tf_op jit(solution)/shard_map/ppermute | solution.py:69
  153.3 12.2 %collective-permute-start.8 = (bf16[2,128,1024]{1,2,0:T(8,128)(2,1)S(1)}, bf16[2,128,1024]{1,2,0:T(8,128)(2,1)S(1)}, u32[]{:S(2)}, u32[]{:S(2)}) collective-permute-start(bf16[2,128,1024]{1,2,0:T(8,128)(2,1)S(1)} %get-tuple-element.78), channel_id=1, source_target_pairs={{0,3},{1,0},{2,1},{3,2},{4,7},{5,4},{6,5},{7,6},{8,11},{9,8},{10,9... | collective-permute-start | bytes 1572872 | tf_op jit(solution)/shard_map/ppermute | solution.py:69
  161.9 4.7 %copy-start.1 = (f32[256,16,128]{2,0,1:T(8,128)}, f32[256,16,128]{2,0,1:T(8,128)S(1)}, u32[]{:S(2)}) copy-start(f32[256,16,128]{2,0,1:T(8,128)S(1)} %bitcast_add_fusion) | copy-start | bytes 6291460
  161.9 13.7 %collective-permute-start.9 = (bf16[2,128,1024]{1,2,0:T(8,128)(2,1)}, bf16[2,128,1024]{1,2,0:T(8,128)(2,1)}, u32[]{:S(2)}, u32[]{:S(2)}) collective-permute-start(bf16[2,128,1024]{1,2,0:T(8,128)(2,1)} %get-tuple-element.79), channel_id=1, source_target_pairs={{0,1},{1,2},{2,3},{3,0},{4,5},{5,6},{6,7},{7,4},{8,9},{9,10},{10,1... | collective-permute-start | bytes 1572872 | tf_op jit(solution)/shard_map/ppermute | solution.py:69
  162.5 13.2 %collective-permute-start.10 = (bf16[2,128,1024]{1,2,0:T(8,128)(2,1)}, bf16[2,128,1024]{1,2,0:T(8,128)(2,1)}, u32[]{:S(2)}, u32[]{:S(2)}) collective-permute-start(bf16[2,128,1024]{1,2,0:T(8,128)(2,1)} %get-tuple-element.77), channel_id=1, source_target_pairs={{0,3},{1,0},{2,1},{3,2},{4,7},{5,4},{6,5},{7,6},{8,11},{9,8},{10,9... | collective-permute-start | bytes 1572872 | tf_op jit(solution)/shard_map/ppermute | solution.py:69
  176.8 2.3 %copy-start.2 = (f32[256,16,128]{2,0,1:T(8,128)S(1)}, f32[256,16,128]{2,0,1:T(8,128)}, u32[]{:S(2)}) copy-start(f32[256,16,128]{2,0,1:T(8,128)} %copy-done.1) | copy-start | bytes 6291460
  180.4 6.1 %copy-start = (f32[256,4096]{1,0:T(8,128)S(1)}, f32[256,4096]{1,0:T(8,128)}, u32[]{:S(2)}) copy-start(f32[256,4096]{1,0:T(8,128)} %fusion.2) | copy-start | bytes 12582916
Sparse Core Ops, SparseCore 0:
  9.0 130.7 all-gather.1
where the time goes:
time: 197 us; the launch traced here: 195 us
  waiting for transfers between devices  100 us (51%)
  matrix products  34 us (17%)
  local copies, waits for them, and re-layouts  18.5 us (9%)
  starting transfers between devices  17.1 us (9%)
  between operations  14 us (7%)
  other arithmetic  11.1 us (6%)
    ppermute x10, waiting for transfers between devices, in_plane(): return lax.ppermute(block, 'ctx', route)  69.4 us
    ppermute x1, waiting for transfers between devices, shards(): lax.ppermute(kv_block, 'ctx', [(i, (i + plane_size) % cycle_size) for i i...  30.3 us
    ppermute x10, starting transfers between devices, in_plane(): return lax.ppermute(block, 'ctx', route)  16.6 us
    dot_general x2, matrix products, shards(): jnp.dot(attn_rows.astype(jnp.bfloat16), gathered_weight[cols], preferred_...  13.7 us
    dot_general x9, matrix products, attend(): jnp.einsum('qhk,khd->qhd', weights.astype(jnp.bfloat16), value_heads, pre...  12.8 us
    unnamed x16, local copies, waits for them, and re-layouts  8.93 us
    dot_general x9, matrix products, attend(): jnp.einsum('qhd,khd->qhk', query_heads, key_heads, preferred_element_type...  7.45 us
    reduce_sum x9, other arithmetic, attend(): denom_new = jnp.sum(weights, axis=2)  6.82 us
  transfers between devices with their start and end apart: 12, of which 4 were waited for; matrix products, arithmetic and copies ran while one was open for 26% of the time, Pallas kernels for 0%

commit v1 on v0

--- a/solution.py
+++ b/solution.py
@@ -15,10 +15,11 @@
     return jnp.sum((positions[:, None] >= utt_ends[None, :]).astype(jnp.int32), axis=1)
 
 
-def attend(carry_state, query_heads, query_seg, kv_block, key_seg):
-    frames = kv_block.shape[1]
-    key_heads = kv_block[0].reshape(frames, -1, HD)
-    value_heads = kv_block[1].reshape(frames, -1, HD)
+def attend(carry_state, query_heads, query_seg, kv_pair, key_seg):
+    keys, values = kv_pair
+    frames = keys.shape[0]
+    key_heads = keys.reshape(frames, -1, HD)
+    value_heads = values.reshape(frames, -1, HD)
     allowed = (query_seg[:, None] == key_seg[None, :])[:, None, :]
     scores = jnp.einsum(
         "qhd,khd->qhk", query_heads, key_heads, preferred_element_type=jnp.float32
@@ -52,6 +53,8 @@
 
     def absorb(carry_state, kv_block, source, heads=slice(None)):
         key_seg = segment_ids(utt_ends, source * frames, frames)
+        if not isinstance(kv_block, tuple):
+            kv_block = (kv_block[0], kv_block[1])
         return attend(carry_state, query_heads[:, heads], query_seg, kv_block, key_seg)
 
     gathered_weight = lax.all_gather(out_weight, "dp", axis=0, tiled=True)
@@ -59,7 +62,6 @@
     plane_size = cycle_size // 2
     plane = cycle_place // plane_size
     spot = cycle_place % plane_size
-    half = frames // 2
 
     def in_plane(block, step):
         route = [
@@ -71,9 +73,7 @@
     def around(block, source_plane):
         ahead = in_plane(block, 1)
         behind = in_plane(block, -1)
-        ahead_two = in_plane(ahead[:, :half], 1)
-        behind_two = in_plane(behind[:, half:], -1)
-        far = jnp.concatenate([ahead_two, behind_two], axis=1)
+        far = (in_plane(ahead[0], 1), in_plane(behind[1], -1))
         base = source_plane * plane_size
         return [
             (ahead, base + (spot - 1) % plane_size),
@@ -103,8 +103,8 @@
         cols = slice(group * width * HD, (group + 1) * width * HD)
         pieces.append(
             (
-                in_plane(partner_ahead[:, :half, cols], 1),
-                in_plane(partner_behind[:, half:, cols], -1),
+                in_plane(partner_ahead[0][:, cols], 1),
+                in_plane(partner_behind[1][:, cols], -1),
             )
         )
     summed = None
@@ -113,7 +113,7 @@
         cols = slice(group * width * HD, (group + 1) * width * HD)
         if summed is not None:
             summed, pieces[group] = lax.optimization_barrier((summed, pieces[group]))
-        far = jnp.concatenate(pieces[group], axis=1)
+        far = pieces[group]
         group_state = tuple(part[:, heads] for part in carry_state)
         max_final, denom_final, numerator = absorb(group_state, far, far_source, heads)
         attn_rows = (numerator / denom_final[:, :, None]).reshape(frames, width * HD)

time: 197 us -> 207 us (1.051)
  waiting for transfers between devices: 100 us -> 113 us
  local copies, waits for them, and re-layouts: 18.5 us -> 15.4 us
  matrix products: 34 us -> 37 us
  starting transfers between devices: 17.1 us -> 14.8 us
    ppermute x10, waiting for transfers between devices: 69.4 us -> 80 us  [in_plane(): return lax.ppermute(block, 'ctx', route)]
    slice x12 -> x5, local copies, waits for them, and re-layouts: 7.48 us -> 3.81 us  [the longest x3 2.08 us: absorb(): kv_block = (kv_block[0], kv_block[1])]
    squeeze x0 -> x2, local copies, waits for them, and re-layouts: none -> 3.49 us  [around(): far = (in_plane(ahead[0], 1), in_plane(behind[1], -1))]
    unnamed x16 -> x13, local copies, waits for them, and re-layouts: 8.93 us -> 5.79 us
    ppermute x10, starting transfers between devices: 16.6 us -> 14.2 us  [in_plane(): return lax.ppermute(block, 'ctx', route)]
  transfers between devices with their start and end apart: 12 -> 12, of which waited for: 4 -> 4; matrix products, arithmetic and copies ran while one was open for 26% -> 25% of each run, Pallas kernels for 0% -> 0%
where the time goes in v1:
time: 207 us; the launch traced here: 206 us
  waiting for transfers between devices  113 us (55%)
  matrix products  37 us (18%)
  local copies, waits for them, and re-layouts  15.4 us (7%)
  starting transfers between devices  14.8 us (7%)
  between operations  13.9 us (7%)
  other arithmetic  12.4 us (6%)
    ppermute x10, waiting for transfers between devices, in_plane(): return lax.ppermute(block, 'ctx', route)  80 us
    ppermute x1, waiting for transfers between devices, shards(): lax.ppermute(kv_block, 'ctx', [(i, (i + plane_size) % cycle_size) for i i...  32.3 us
    dot_general x9, matrix products, attend(): jnp.einsum('qhk,khd->qhd', weights.astype(jnp.bfloat16), value_heads, pre...  14.6 us
    ppermute x10, starting transfers between devices, in_plane(): return lax.ppermute(block, 'ctx', route)  14.2 us
    dot_general x2, matrix products, shards(): jnp.dot(attn_rows.astype(jnp.bfloat16), gathered_weight[cols], preferred_...  13.9 us
    dot_general x9, matrix products, attend(): jnp.einsum('qhd,khd->qhk', query_heads, key_heads, preferred_element_type...  8.5 us
    reduce_sum x9, other arithmetic, attend(): denom_new = jnp.sum(weights, axis=2)  6.81 us
    unnamed x13, local copies, waits for them, and re-layouts  5.79 us
  transfers between devices with their start and end apart: 12, of which 4 were waited for; matrix products, arithmetic and copies ran while one was open for 25% of the time, Pallas kernels for 0%

profile of v1, /device:TPU:102, one launch (start us, length us, event | category | flops | bytes accessed | tf_op | source)
XLA Modules:
  0.0 206.4 jit_solution(16548473643465508391)
XLA Ops:
  7.3 1.5 copy.81
  8.8 2.4 %copy.80 = bf16[1,256,2048]{1,2,0:T(8,128)(2,1)} copy(bf16[1,256,2048]{2,1,0:T(8,128)(2,1)} %param.6) | data formatting | bytes 2097152 | tf_op args[1]
  11.1 2.8 %pad_maximum_fusion = bf16[2,256,2048]{1,2,0:T(8,128)(2,1)} fusion(bf16[1,256,2048]{1,2,0:T(8,128)(2,1)S(1)} %copy.81, bf16[1,256,2048]{1,2,0:T(8,128)(2,1)} %copy.80), kind=kLoop, calls=%fused_computation.48 | loop fusion | flops 1048576 | bytes 4194304 | tf_op jit(solution)/shard_map/concatenate | solution.py:61
  14.0 1.6 collective-permute-start
  16.1 1.7 collective-permute-start.1
  17.8 1.5 copy.75
  21.5 1.4 fusion.72
  23.8 39.1 %collective-permute-done = bf16[2,256,2048]{1,2,0:T(8,128)(2,1)} collective-permute-done((bf16[2,256,2048]{1,2,0:T(8,128)(2,1)}, bf16[2,256,2048]{1,2,0:T(8,128)(2,1)}, u32[]{:S(2)}, u32[]{:S(2)}) %collective-permute-start) | collective-permute-done | bytes 2097184 | tf_op jit(solution)/shard_map/ppermute | solution.py:71
  62.9 1.7 slice_bitcast_fusion.3
  66.5 1.5 bitcast_add_fusion.5
  68.5 1.7 slice_bitcast_fusion.2
  70.2 3.2 %collective-permute-start.3 = (bf16[256,2048]{0,1:T(8,128)(2,1)S(1)}, bf16[256,2048]{0,1:T(8,128)(2,1)S(1)}, u32[]{:S(2)}, u32[]{:S(2)}) collective-permute-start(bf16[256,2048]{0,1:T(8,128)(2,1)S(1)} %get-tuple-element.85), channel_id=1, source_target_pairs={{0,3},{1,0},{2,1},{3,2},{4,7},{5,4},{6,5},{7,6},{8,11},{9,8},{10,9... | collective-permute-start | bytes 3145736 | tf_op jit(solution)/shard_map/ppermute | solution.py:71
  75.2 1.5 bitcast_add_fusion.4
  76.8 32.3 %collective-permute-done.4 = bf16[2,256,2048]{1,2,0:T(8,128)(2,1)} collective-permute-done((bf16[2,256,2048]{1,2,0:T(8,128)(2,1)}, bf16[2,256,2048]{1,2,0:T(8,128)(2,1)}, u32[]{:S(2)}, u32[]{:S(2)}) %collective-permute-start.4) | collective-permute-done | bytes 2097184 | tf_op jit(solution)/shard_map/ppermute | solution.py:84
  109.0 1.7 fusion.118
  112.4 1.4 collective-permute-start.5
  115.6 1.5 bitcast_add_fusion.3
  118.1 1.5 bitcast_add_fusion.2
  119.6 37.0 %collective-permute-done.6 = bf16[2,256,2048]{1,2,0:T(8,128)(2,1)S(1)} collective-permute-done((bf16[2,256,2048]{1,2,0:T(8,128)(2,1)}, bf16[2,256,2048]{1,2,0:T(8,128)(2,1)S(1)}, u32[]{:S(2)}, u32[]{:S(2)}) %collective-permute-start.6) | collective-permute-done | bytes 2097184 | tf_op jit(solution)/shard_map/ppermute | solution.py:71
  159.8 1.1 collective-permute-start.7
  162.7 1.5 bitcast_add_fusion.1
  166.1 1.5 bitcast_add_fusion
  167.6 1.7 collective-permute-start.9
  169.3 1.6 collective-permute-start.10
  170.9 3.8 %collective-permute-done.7 = bf16[256,1024]{0,1:T(8,128)(2,1)S(1)} collective-permute-done((bf16[256,1024]{0,1:T(8,128)(2,1)S(1)}, bf16[256,1024]{0,1:T(8,128)(2,1)S(1)}, u32[]{:S(2)}, u32[]{:S(2)}) %collective-permute-start.7) | collective-permute-done | bytes 524320 | tf_op jit(solution)/shard_map/ppermute | solution.py:71
  175.6 1.8 fusion.91
  177.4 2.1 %copy.110 = bf16[256,8,128]{0,2,1:T(8,128)(2,1)} copy(bf16[256,8,128]{2,0,1:T(8,128)(2,1)} %fusion.91) | data formatting | bytes 1048576 | tf_op jit(solution)/shard_map/convert_element_type | solution.py:121
  179.5 7.9 %fusion.2 = f32[256,4096]{1,0:T(8,128)} fusion(bf16[256,1024]{0,1:T(8,128)(2,1)} %bitcast.199, bf16[2048,4096]{1,0:T(8,128)(2,1)} %all-gather.2.cloned.1.call-done), kind=kOutput, calls=%fused_computation.2 | convolution fusion | flops 2147483648 | bytes 13107200 | tf_op jit(solution)/shard_map/dot_general | solution.py:120
  187.4 1.6 fusion.122
  189.3 2.2 %fusion.92 = bf16[256,8,128]{2,0,1:T(8,128)(2,1)S(1)} fusion(bf16[256,8,128]{0,2,1:T(8,128)(2,1)} %bitcast.40, f32[256,8,256]{0,2,1:T(8,128)S(1)} %get-tuple-element.120, f32[256,8]{0,1:T(8,128)S(1)} %slice_maximum_fusion, f32[256,16,128]{2,0,1:T(8,128)S(1)} %bitcast_add_fusion, f32[256,8]{0,1:T(8,128)S(1)} %get-tuple-element.61, ...), kind=kOutput, calls=%fused_computation.99 | convolution fusion | flops 136314880 | bytes 4218880 | tf_op jit(solution)/shard_map/qhk,khd->qhd/dot_general | solution.py:32
  191.7 6.0 %fusion = f32[256,4096]{1,0:T(8,128)S(1)} fusion(bf16[256,1024]{0,1:T(8,128)(2,1)S(1)} %bitcast.200, bf16[2048,4096]{1,0:T(8,128)(2,1)} %all-gather.2.cloned.1.call-done), kind=kOutput, calls=%fused_computation | convolution fusion | flops 2147483648 | bytes 13107200 | tf_op jit(solution)/shard_map/dot_general | solution.py:120
  197.7 1.8 fusion.39
  (69 shorter events, 20.8 us)
Async XLA Ops:
  6.5 172.9 %all-gather.2.cloned.1.call-start = ((), (), s32[]{:S(2)}) async-start(), calls=%async_computation | async-start | bytes 17825792 | tf_op jit(solution)/shard_map/all_gather | solution.py:60
  8.7 10.5 %copy-start.3 = (s32[1,8]{1,0:T(1,128)S(1)}, s32[1,8]{1,0:T(1,128)}, u32[]{:S(2)}) copy-start(s32[1,8]{1,0:T(1,128)} %param.8) | copy-start | bytes 100
  8.8 10.7 %copy-start.1 = (bf16[1,256,2048]{2,1,0:T(8,128)(2,1)S(1)}, bf16[1,256,2048]{2,1,0:T(8,128)(2,1)}, u32[]{:S(2)}) copy-start(bf16[1,256,2048]{2,1,0:T(8,128)(2,1)} %param.6) | copy-start | bytes 3145732
  11.1 8.5 %copy-start.2 = (bf16[1,256,2048]{2,1,0:T(8,128)(2,1)S(1)}, bf16[1,256,2048]{2,1,0:T(8,128)(2,1)}, u32[]{:S(2)}) copy-start(bf16[1,256,2048]{2,1,0:T(8,128)(2,1)} %param.7) | copy-start | bytes 3145732
  14.0 49.0 %collective-permute-start = (bf16[2,256,2048]{1,2,0:T(8,128)(2,1)}, bf16[2,256,2048]{1,2,0:T(8,128)(2,1)}, u32[]{:S(2)}, u32[]{:S(2)}) collective-permute-start(bf16[2,256,2048]{1,2,0:T(8,128)(2,1)} %pad_maximum_fusion), channel_id=1, source_target_pairs={{0,1},{1,2},{2,3},{3,0},{4,5},{5,6},{6,7},{7,4},{8,9},{9,10},{10,1... | collective-permute-start | bytes 6291464 | tf_op jit(solution)/shard_map/ppermute | solution.py:71
  15.5 93.5 %collective-permute-start.4 = (bf16[2,256,2048]{1,2,0:T(8,128)(2,1)}, bf16[2,256,2048]{1,2,0:T(8,128)(2,1)}, u32[]{:S(2)}, u32[]{:S(2)}) collective-permute-start(bf16[2,256,2048]{1,2,0:T(8,128)(2,1)} %pad_maximum_fusion), channel_id=1, source_target_pairs={{0,4},{1,5},{2,6},{3,7},{4,0},{5,1},{6,2},{7,3},{8,12},{9,13},{10,... | collective-permute-start | bytes 6291464 | tf_op jit(solution)/shard_map/ppermute | solution.py:84
  16.1 52.4 %collective-permute-start.1 = (bf16[2,256,2048]{1,2,0:T(8,128)(2,1)}, bf16[2,256,2048]{1,2,0:T(8,128)(2,1)}, u32[]{:S(2)}, u32[]{:S(2)}) collective-permute-start(bf16[2,256,2048]{1,2,0:T(8,128)(2,1)} %pad_maximum_fusion), channel_id=1, source_target_pairs={{0,3},{1,0},{2,1},{3,2},{4,7},{5,4},{6,5},{7,6},{8,11},{9,8},{10,9... | collective-permute-start | bytes 6291464 | tf_op jit(solution)/shard_map/ppermute | solution.py:71
  68.1 45.7 %collective-permute-start.2 = (bf16[256,2048]{0,1:T(8,128)(2,1)S(1)}, bf16[256,2048]{0,1:T(8,128)(2,1)S(1)}, u32[]{:S(2)}, u32[]{:S(2)}) collective-permute-start(bf16[256,2048]{0,1:T(8,128)(2,1)S(1)} %get-tuple-element.88), channel_id=1, source_target_pairs={{0,1},{1,2},{2,3},{3,0},{4,5},{5,6},{6,7},{7,4},{8,9},{9,10},{10,1... | collective-permute-start | bytes 3145736 | tf_op jit(solution)/shard_map/ppermute | solution.py:71
  70.2 45.4 %collective-permute-start.3 = (bf16[256,2048]{0,1:T(8,128)(2,1)S(1)}, bf16[256,2048]{0,1:T(8,128)(2,1)S(1)}, u32[]{:S(2)}, u32[]{:S(2)}) collective-permute-start(bf16[256,2048]{0,1:T(8,128)(2,1)S(1)} %get-tuple-element.85), channel_id=1, source_target_pairs={{0,3},{1,0},{2,1},{3,2},{4,7},{5,4},{6,5},{7,6},{8,11},{9,8},{10,9... | collective-permute-start | bytes 3145736 | tf_op jit(solution)/shard_map/ppermute | solution.py:71
  111.6 45.0 %collective-permute-start.6 = (bf16[2,256,2048]{1,2,0:T(8,128)(2,1)}, bf16[2,256,2048]{1,2,0:T(8,128)(2,1)S(1)}, u32[]{:S(2)}, u32[]{:S(2)}) collective-permute-start(bf16[2,256,2048]{1,2,0:T(8,128)(2,1)} %collective-permute-done.4), channel_id=1, source_target_pairs={{0,3},{1,0},{2,1},{3,2},{4,7},{5,4},{6,5},{7,6},{8,11},{9,8},{10,9... | collective-permute-start | bytes 6291464 | tf_op jit(solution)/shard_map/ppermute | solution.py:71
  112.4 46.3 %collective-permute-start.5 = (bf16[2,256,2048]{1,2,0:T(8,128)(2,1)}, bf16[2,256,2048]{1,2,0:T(8,128)(2,1)S(1)}, u32[]{:S(2)}, u32[]{:S(2)}) collective-permute-start(bf16[2,256,2048]{1,2,0:T(8,128)(2,1)} %collective-permute-done.4), channel_id=1, source_target_pairs={{0,1},{1,2},{2,3},{3,0},{4,5},{5,6},{6,7},{7,4},{8,9},{9,10},{10,1... | collective-permute-start | bytes 6291464 | tf_op jit(solution)/shard_map/ppermute | solution.py:71
  157.7 17.9 %collective-permute-start.8 = (bf16[256,1024]{0,1:T(8,128)(2,1)S(1)}, bf16[256,1024]{0,1:T(8,128)(2,1)S(1)}, u32[]{:S(2)}, u32[]{:S(2)}) collective-permute-start(bf16[256,1024]{0,1:T(8,128)(2,1)S(1)} %get-tuple-element.92), channel_id=1, source_target_pairs={{0,3},{1,0},{2,1},{3,2},{4,7},{5,4},{6,5},{7,6},{8,11},{9,8},{10,9... | collective-permute-start | bytes 1572872 | tf_op jit(solution)/shard_map/ppermute | solution.py:71
  159.8 15.0 %collective-permute-start.7 = (bf16[256,1024]{0,1:T(8,128)(2,1)S(1)}, bf16[256,1024]{0,1:T(8,128)(2,1)S(1)}, u32[]{:S(2)}, u32[]{:S(2)}) collective-permute-start(bf16[256,1024]{0,1:T(8,128)(2,1)S(1)} %get-tuple-element.94), channel_id=1, source_target_pairs={{0,1},{1,2},{2,3},{3,0},{4,5},{5,6},{6,7},{7,4},{8,9},{9,10},{10,1... | collective-permute-start | bytes 1572872 | tf_op jit(solution)/shard_map/ppermute | solution.py:71
  167.6 19.7 %collective-permute-start.9 = (bf16[256,1024]{0,1:T(8,128)(2,1)}, bf16[256,1024]{0,1:T(8,128)(2,1)}, u32[]{:S(2)}, u32[]{:S(2)}) collective-permute-start(bf16[256,1024]{0,1:T(8,128)(2,1)} %get-tuple-element.93), channel_id=1, source_target_pairs={{0,1},{1,2},{2,3},{3,0},{4,5},{5,6},{6,7},{7,4},{8,9},{9,10},{10,1... | collective-permute-start | bytes 1572872 | tf_op jit(solution)/shard_map/ppermute | solution.py:71
  169.3 18.0 %collective-permute-start.10 = (bf16[256,1024]{0,1:T(8,128)(2,1)}, bf16[256,1024]{0,1:T(8,128)(2,1)}, u32[]{:S(2)}, u32[]{:S(2)}) collective-permute-start(bf16[256,1024]{0,1:T(8,128)(2,1)} %get-tuple-element.91), channel_id=1, source_target_pairs={{0,3},{1,0},{2,1},{3,2},{4,7},{5,4},{6,5},{7,6},{8,11},{9,8},{10,9... | collective-permute-start | bytes 1572872 | tf_op jit(solution)/shard_map/ppermute | solution.py:71
  191.7 6.1 %copy-start = (f32[256,4096]{1,0:T(8,128)S(1)}, f32[256,4096]{1,0:T(8,128)}, u32[]{:S(2)}) copy-start(f32[256,4096]{1,0:T(8,128)} %fusion.2) | copy-start | bytes 12582916
Sparse Core Ops, SparseCore 0:
  9.0 132.9 all-gather.1

commit v2 on v0

--- a/solution.py
+++ b/solution.py
@@ -116,10 +116,11 @@
         far = jnp.concatenate(pieces[group], axis=1)
         group_state = tuple(part[:, heads] for part in carry_state)
         max_final, denom_final, numerator = absorb(group_state, far, far_source, heads)
-        attn_rows = (numerator / denom_final[:, :, None]).reshape(frames, width * HD)
-        partial = jnp.dot(
-            attn_rows.astype(jnp.bfloat16),
-            gathered_weight[cols],
+        attn_heads = (numerator / denom_final[:, :, None]).astype(jnp.bfloat16)
+        partial = jnp.einsum(
+            "qhd,hdn->qn",
+            attn_heads,
+            gathered_weight[cols].reshape(width, HD, -1),
             preferred_element_type=jnp.float32,
         )
         summed = partial if summed is None else summed + partial

time: 197 us -> 221 us (1.12)
  local copies, waits for them, and re-layouts: 18.5 us -> 31.2 us
  waiting for transfers between devices: 100 us -> 107 us
  other arithmetic: 11.1 us -> 14.5 us
  matrix products: 34 us -> 36.7 us
    slice x0 -> x1, local copies, waits for them, and re-layouts: none -> 11.7 us  [shards(): gathered_weight[cols].reshape(width, HD, -1)]
    dot_general x2, matrix products: 13.7 us -> 17.7 us  [shards(): jnp.einsum('qhd,hdn->qn', attn_heads, gathered_weight[cols].reshape(width...]
    ppermute x10, waiting for transfers between devices: 69.4 us -> 72.9 us  [in_plane(): return lax.ppermute(block, 'ctx', route)]
    broadcast_in_dim x1, other arithmetic: 1.83 us -> 5.3 us  [shards(): return summed.astype(jnp.bfloat16)[None]]
    ppermute x1, waiting for transfers between devices: 30.3 us -> 33.4 us  [shards(): lax.ppermute(kv_block, 'ctx', [(i, (i + plane_size) % cycle_size) for i i...]
    dot_general x9 -> x7, matrix products: 12.8 us -> 11.6 us  [attend(): jnp.einsum('qhk,khd->qhd', weights.astype(jnp.bfloat16), value_heads, pre...]
    unnamed x16 -> x10, local copies, waits for them, and re-layouts: 8.93 us -> 8.9 us
  transfers between devices with their start and end apart: 12 -> 12, of which waited for: 4 -> 5; matrix products, arithmetic and copies ran while one was open for 26% -> 29% of each run, Pallas kernels for 0% -> 0%
where the time goes in v2:
time: 221 us; the launch traced here: 219 us
  waiting for transfers between devices  107 us (48%)
  matrix products  36.7 us (17%)
  local copies, waits for them, and re-layouts  31.2 us (14%)
  starting transfers between devices  15.8 us (7%)
  other arithmetic  14.5 us (7%)
  between operations  13.9 us (6%)
    ppermute x10, waiting for transfers between devices, in_plane(): return lax.ppermute(block, 'ctx', route)  72.9 us
    ppermute x1, waiting for transfers between devices, shards(): lax.ppermute(kv_block, 'ctx', [(i, (i + plane_size) % cycle_size) for i i...  33.4 us
    dot_general x2, matrix products, shards(): jnp.einsum('qhd,hdn->qn', attn_heads, gathered_weight[cols].reshape(width...  17.7 us
    ppermute x10, starting transfers between devices, in_plane(): return lax.ppermute(block, 'ctx', route)  15.3 us
    slice x1, local copies, waits for them, and re-layouts, shards(): gathered_weight[cols].reshape(width, HD, -1)  11.7 us
    dot_general x7, matrix products, attend(): jnp.einsum('qhk,khd->qhd', weights.astype(jnp.bfloat16), value_heads, pre...  11.6 us
    unnamed x10, local copies, waits for them, and re-layouts  8.9 us
    dot_general x9, matrix products, attend(): jnp.einsum('qhd,khd->qhk', query_heads, key_heads, preferred_element_type...  7.46 us
  transfers between devices with their start and end apart: 12, of which 5 were waited for; matrix products, arithmetic and copies ran while one was open for 29% of the time, Pallas kernels for 0%

profile of v2, /device:TPU:102, one launch (start us, length us, event | category | flops | bytes accessed | tf_op | source)
XLA Modules:
  0.0 219.2 jit_solution(14079075099310781645)
XLA Ops:
  7.3 1.5 copy.67
  8.8 1.5 copy.68
  10.2 1.5 pad_maximum_fusion
  11.7 1.6 collective-permute-start
  13.3 1.7 collective-permute-start.1
  15.7 1.5 copy.62
  17.2 1.5 copy.135
  18.7 1.6 copy.136
  21.8 1.4 fusion.68
  24.1 36.6 %collective-permute-done = bf16[2,256,2048]{1,2,0:T(8,128)(2,1)} collective-permute-done((bf16[2,256,2048]{1,2,0:T(8,128)(2,1)}, bf16[2,256,2048]{1,2,0:T(8,128)(2,1)}, u32[]{:S(2)}, u32[]{:S(2)}) %collective-permute-start) | collective-permute-done | bytes 2097184 | tf_op jit(solution)/shard_map/ppermute | solution.py:69
  60.7 1.7 fusion.128
  64.3 1.5 bitcast_add_fusion.5
  65.8 1.3 slice.132
  69.6 1.5 bitcast_add_fusion.4
  71.2 3.1 %collective-permute-start.3 = (bf16[2,128,2048]{1,2,0:T(8,128)(2,1)S(1)}, bf16[2,128,2048]{1,2,0:T(8,128)(2,1)S(1)}, u32[]{:S(2)}, u32[]{:S(2)}) collective-permute-start(bf16[2,128,2048]{1,2,0:T(8,128)(2,1)S(1)} %slice.133), channel_id=1, source_target_pairs={{0,3},{1,0},{2,1},{3,2},{4,7},{5,4},{6,5},{7,6},{8,11},{9,8},{10,9... | collective-permute-start | bytes 3145736 | tf_op jit(solution)/shard_map/ppermute | solution.py:69
  74.3 33.4 %collective-permute-done.4 = bf16[2,256,2048]{1,2,0:T(8,128)(2,1)} collective-permute-done((bf16[2,256,2048]{1,2,0:T(8,128)(2,1)}, bf16[2,256,2048]{1,2,0:T(8,128)(2,1)}, u32[]{:S(2)}, u32[]{:S(2)}) %collective-permute-start.4) | collective-permute-done | bytes 2097184 | tf_op jit(solution)/shard_map/ppermute | solution.py:84
  107.7 3.2 %collective-permute-start.6 = (bf16[2,256,2048]{1,2,0:T(8,128)(2,1)}, bf16[2,256,2048]{1,2,0:T(8,128)(2,1)S(1)}, u32[]{:S(2)}, u32[]{:S(2)}) collective-permute-start(bf16[2,256,2048]{1,2,0:T(8,128)(2,1)} %collective-permute-done.4), channel_id=1, source_target_pairs={{0,3},{1,0},{2,1},{3,2},{4,7},{5,4},{6,5},{7,6},{8,11},{9,8},{10,9... | collective-permute-start | bytes 6291464 | tf_op jit(solution)/shard_map/ppermute | solution.py:69
  110.9 1.7 fusion.125
  116.0 1.5 bitcast_add_fusion.3
  118.5 1.5 bitcast_add_fusion.2
  120.0 31.9 %collective-permute-done.5 = bf16[2,256,2048]{1,2,0:T(8,128)(2,1)S(1)} collective-permute-done((bf16[2,256,2048]{1,2,0:T(8,128)(2,1)}, bf16[2,256,2048]{1,2,0:T(8,128)(2,1)S(1)}, u32[]{:S(2)}, u32[]{:S(2)}) %collective-permute-start.5) | collective-permute-done | bytes 2097184 | tf_op jit(solution)/shard_map/ppermute | solution.py:69
  153.9 1.5 bitcast_add_fusion.1
  157.4 3.2 %collective-permute-start.8 = (bf16[2,128,1024]{1,2,0:T(8,128)(2,1)S(1)}, bf16[2,128,1024]{1,2,0:T(8,128)(2,1)S(1)}, u32[]{:S(2)}, u32[]{:S(2)}) collective-permute-start(bf16[2,128,1024]{1,2,0:T(8,128)(2,1)S(1)} %get-tuple-element.80), channel_id=1, source_target_pairs={{0,3},{1,0},{2,1},{3,2},{4,7},{5,4},{6,5},{7,6},{8,11},{9,8},{10,9... | collective-permute-start | bytes 1572872 | tf_op jit(solution)/shard_map/ppermute | solution.py:69
  162.6 2.5 %bitcast_add_fusion = f32[256,16,128]{2,0,1:T(8,128)} fusion(f32[256,16,128]{2,0,1:T(8,128)S(1)} %bitcast_add_fusion.1, bf16[256,16,128]{0,2,1:T(8,128)(2,1)S(1)} %bitcast.189, f32[16,256,256]{2,1,0:T(8,128)S(1)} %get-tuple-element.122, f32[256,16]{0,1:T(8,128)S(1)} %max.29, pred[256,256]{0,1:T(8,128)(4,1)S(1)} %get-tuple-element.99, ...), kind=kOutput, calls=%fused_computation.49 | convolution fusion | flops 273678336 | bytes 9535488 | tf_op jit(solution)/shard_map/qhk,khd->qhd/dot_general | solution.py:31
  165.1 2.0 collective-permute-start.9
  167.1 3.5 %collective-permute-done.7 = bf16[2,128,1024]{1,2,0:T(8,128)(2,1)S(1)} collective-permute-done((bf16[2,128,1024]{1,2,0:T(8,128)(2,1)S(1)}, bf16[2,128,1024]{1,2,0:T(8,128)(2,1)S(1)}, u32[]{:S(2)}, u32[]{:S(2)}) %collective-permute-start.7) | collective-permute-done | bytes 524320 | tf_op jit(solution)/shard_map/ppermute | solution.py:69
  173.6 11.7 %fusion.120 = (bf16[1024,4096]{1,0:T(8,128)(2,1)}, bf16[1024,4096]{1,0:T(8,128)(2,1)}) fusion(bf16[2048,4096]{1,0:T(8,128)(2,1)} %all-gather.2.cloned.1.call-done), kind=kLoop, calls=%fused_computation.171 | loop fusion | bytes 33554432 | tf_op jit(solution)/shard_map/slice | solution.py:123
  185.2 8.8 %convolution_bitcast_fusion.1 = f32[256,4096]{1,0:T(8,128)} fusion(bf16[8,128,4096]{2,1,0:T(8,128)(2,1)} %bitcast.183, bf16[256,8,128]{0,2,1:T(8,128)(2,1)} %bitcast.202, f32[256,8,256]{0,2,1:T(8,128)S(1)} %get-tuple-element.108, f32[256,8]{0,1:T(8,128)S(1)} %slice_maximum_fusion.1, f32[256,16,128]{2,0,1:T(8,128)} %bitcast_add_fusion, ...), kind=kOutput, calls=%fused_computation.1 | convolution fusion | flops 2283798528 | bytes 16277504 | tf_op jit(solution)/shard_map/qhd,hdn->qn/dot_general | solution.py:120
  194.1 1.1 constant_dynamic-update-slice_fusion.5
  195.2 1.2 constant_dynamic-update-slice_fusion.4
  198.1 8.9 %convolution_bitcast_fusion = f32[256,4096]{1,0:T(8,128)} fusion(bf16[8,128,4096]{2,1,0:T(8,128)(2,1)} %bitcast.182, bf16[256,8,128]{0,2,1:T(8,128)(2,1)} %bitcast.203, f32[256,8,256]{0,2,1:T(8,128)S(1)} %get-tuple-element.124, f32[256,8]{0,1:T(8,128)S(1)} %slice_maximum_fusion, f32[256,16,128]{2,0,1:T(8,128)} %bitcast_add_fusion, ...), kind=kOutput, calls=%fused_computation | convolution fusion | flops 2283798528 | bytes 16277504 | tf_op jit(solution)/shard_map/qhd,hdn->qn/dot_general | solution.py:120
  207.0 5.3 %fusion.35 = bf16[1,256,4096]{2,1,0:T(8,128)(2,1)} fusion(f32[256,4096]{1,0:T(8,128)} %convolution_bitcast_fusion.1, f32[256,4096]{1,0:T(8,128)} %convolution_bitcast_fusion), kind=kLoop, calls=%fused_computation.45 | loop fusion | flops 2097152 | bytes 10485760 | tf_op jit(solution)/shard_map/broadcast_in_dim | solution.py:127
  (71 shorter events, 22.9 us)
Async XLA Ops:
  6.5 167.0 %all-gather.2.cloned.1.call-start = ((), (), s32[]{:S(2)}) async-start(), calls=%async_computation | async-start | bytes 17825792 | tf_op jit(solution)/shard_map/all_gather | solution.py:57
  7.3 8.3 %copy-start = (s32[1,8]{1,0:T(1,128)S(1)}, s32[1,8]{1,0:T(1,128)}, u32[]{:S(2)}) copy-start(s32[1,8]{1,0:T(1,128)} %param.8) | copy-start | bytes 100
  11.7 49.0 %collective-permute-start = (bf16[2,256,2048]{1,2,0:T(8,128)(2,1)}, bf16[2,256,2048]{1,2,0:T(8,128)(2,1)}, u32[]{:S(2)}, u32[]{:S(2)}) collective-permute-start(bf16[2,256,2048]{1,2,0:T(8,128)(2,1)} %pad_maximum_fusion), channel_id=1, source_target_pairs={{0,1},{1,2},{2,3},{3,0},{4,5},{5,6},{6,7},{7,4},{8,9},{9,10},{10,1... | collective-permute-start | bytes 6291464 | tf_op jit(solution)/shard_map/ppermute | solution.py:69
  13.3 54.3 %collective-permute-start.1 = (bf16[2,256,2048]{1,2,0:T(8,128)(2,1)}, bf16[2,256,2048]{1,2,0:T(8,128)(2,1)S(1)}, u32[]{:S(2)}, u32[]{:S(2)}) collective-permute-start(bf16[2,256,2048]{1,2,0:T(8,128)(2,1)} %pad_maximum_fusion), channel_id=1, source_target_pairs={{0,3},{1,0},{2,1},{3,2},{4,7},{5,4},{6,5},{7,6},{8,11},{9,8},{10,9... | collective-permute-start | bytes 6291464 | tf_op jit(solution)/shard_map/ppermute | solution.py:69
  15.0 92.7 %collective-permute-start.4 = (bf16[2,256,2048]{1,2,0:T(8,128)(2,1)}, bf16[2,256,2048]{1,2,0:T(8,128)(2,1)}, u32[]{:S(2)}, u32[]{:S(2)}) collective-permute-start(bf16[2,256,2048]{1,2,0:T(8,128)(2,1)} %pad_maximum_fusion), channel_id=1, source_target_pairs={{0,4},{1,5},{2,6},{3,7},{4,0},{5,1},{6,2},{7,3},{8,12},{9,13},{10,... | collective-permute-start | bytes 6291464 | tf_op jit(solution)/shard_map/ppermute | solution.py:84
  67.2 46.4 %collective-permute-start.2 = (bf16[2,128,2048]{1,2,0:T(8,128)(2,1)S(1)}, bf16[2,128,2048]{1,2,0:T(8,128)(2,1)S(1)}, u32[]{:S(2)}, u32[]{:S(2)}) collective-permute-start(bf16[2,128,2048]{1,2,0:T(8,128)(2,1)S(1)} %slice.132), channel_id=1, source_target_pairs={{0,1},{1,2},{2,3},{3,0},{4,5},{5,6},{6,7},{7,4},{8,9},{9,10},{10,1... | collective-permute-start | bytes 3145736 | tf_op jit(solution)/shard_map/ppermute | solution.py:69
  71.2 42.5 %collective-permute-start.3 = (bf16[2,128,2048]{1,2,0:T(8,128)(2,1)S(1)}, bf16[2,128,2048]{1,2,0:T(8,128)(2,1)S(1)}, u32[]{:S(2)}, u32[]{:S(2)}) collective-permute-start(bf16[2,128,2048]{1,2,0:T(8,128)(2,1)S(1)} %slice.133), channel_id=1, source_target_pairs={{0,3},{1,0},{2,1},{3,2},{4,7},{5,4},{6,5},{7,6},{8,11},{9,8},{10,9... | collective-permute-start | bytes 3145736 | tf_op jit(solution)/shard_map/ppermute | solution.py:69
  107.7 44.2 %collective-permute-start.5 = (bf16[2,256,2048]{1,2,0:T(8,128)(2,1)}, bf16[2,256,2048]{1,2,0:T(8,128)(2,1)S(1)}, u32[]{:S(2)}, u32[]{:S(2)}) collective-permute-start(bf16[2,256,2048]{1,2,0:T(8,128)(2,1)} %collective-permute-done.4), channel_id=1, source_target_pairs={{0,1},{1,2},{2,3},{3,0},{4,5},{5,6},{6,7},{7,4},{8,9},{9,10},{10,1... | collective-permute-start | bytes 6291464 | tf_op jit(solution)/shard_map/ppermute | solution.py:69
  107.7 48.7 %collective-permute-start.6 = (bf16[2,256,2048]{1,2,0:T(8,128)(2,1)}, bf16[2,256,2048]{1,2,0:T(8,128)(2,1)S(1)}, u32[]{:S(2)}, u32[]{:S(2)}) collective-permute-start(bf16[2,256,2048]{1,2,0:T(8,128)(2,1)} %collective-permute-done.4), channel_id=1, source_target_pairs={{0,3},{1,0},{2,1},{3,2},{4,7},{5,4},{6,5},{7,6},{8,11},{9,8},{10,9... | collective-permute-start | bytes 6291464 | tf_op jit(solution)/shard_map/ppermute | solution.py:69
  156.4 14.3 %collective-permute-start.7 = (bf16[2,128,1024]{1,2,0:T(8,128)(2,1)S(1)}, bf16[2,128,1024]{1,2,0:T(8,128)(2,1)S(1)}, u32[]{:S(2)}, u32[]{:S(2)}) collective-permute-start(bf16[2,128,1024]{1,2,0:T(8,128)(2,1)S(1)} %get-tuple-element.82), channel_id=1, source_target_pairs={{0,1},{1,2},{2,3},{3,0},{4,5},{5,6},{6,7},{7,4},{8,9},{9,10},{10,1... | collective-permute-start | bytes 1572872 | tf_op jit(solution)/shard_map/ppermute | solution.py:69
  157.4 14.3 %collective-permute-start.8 = (bf16[2,128,1024]{1,2,0:T(8,128)(2,1)S(1)}, bf16[2,128,1024]{1,2,0:T(8,128)(2,1)S(1)}, u32[]{:S(2)}, u32[]{:S(2)}) collective-permute-start(bf16[2,128,1024]{1,2,0:T(8,128)(2,1)S(1)} %get-tuple-element.80), channel_id=1, source_target_pairs={{0,3},{1,0},{2,1},{3,2},{4,7},{5,4},{6,5},{7,6},{8,11},{9,8},{10,9... | collective-permute-start | bytes 1572872 | tf_op jit(solution)/shard_map/ppermute | solution.py:69
  165.1 29.0 %collective-permute-start.10 = (bf16[2,128,1024]{1,2,0:T(8,128)(2,1)}, bf16[2,128,1024]{1,2,0:T(8,128)(2,1)}, u32[]{:S(2)}, u32[]{:S(2)}) collective-permute-start(bf16[2,128,1024]{1,2,0:T(8,128)(2,1)} %get-tuple-element.79), channel_id=1, source_target_pairs={{0,3},{1,0},{2,1},{3,2},{4,7},{5,4},{6,5},{7,6},{8,11},{9,8},{10,9... | collective-permute-start | bytes 1572872 | tf_op jit(solution)/shard_map/ppermute | solution.py:69
  165.1 29.0 %collective-permute-start.9 = (bf16[2,128,1024]{1,2,0:T(8,128)(2,1)}, bf16[2,128,1024]{1,2,0:T(8,128)(2,1)}, u32[]{:S(2)}, u32[]{:S(2)}) collective-permute-start(bf16[2,128,1024]{1,2,0:T(8,128)(2,1)} %get-tuple-element.81), channel_id=1, source_target_pairs={{0,1},{1,2},{2,3},{3,0},{4,5},{5,6},{6,7},{7,4},{8,9},{9,10},{10,1... | collective-permute-start | bytes 1572872 | tf_op jit(solution)/shard_map/ppermute | solution.py:69
Sparse Core Ops, SparseCore 0:
  9.0 132.1 all-gather.1

commit v3 on v0

--- a/solution.py
+++ b/solution.py
@@ -96,11 +96,11 @@
     for block, source in arrivals:
         carry_state = lax.optimization_barrier(absorb(carry_state, block, source))
     far_source = (1 - plane) * plane_size + (spot + 2) % plane_size
-    groups = 2
-    width = HQ // groups
+    bounds = (0, HQ * 3 // 4, HQ)
+    groups = len(bounds) - 1
     pieces = []
     for group in range(groups):
-        cols = slice(group * width * HD, (group + 1) * width * HD)
+        cols = slice(bounds[group] * HD, bounds[group + 1] * HD)
         pieces.append(
             (
                 in_plane(partner_ahead[:, :half, cols], 1),
@@ -109,14 +109,14 @@
         )
     summed = None
     for group in range(groups):
-        heads = slice(group * width, (group + 1) * width)
-        cols = slice(group * width * HD, (group + 1) * width * HD)
+        heads = slice(bounds[group], bounds[group + 1])
+        cols = slice(bounds[group] * HD, bounds[group + 1] * HD)
         if summed is not None:
             summed, pieces[group] = lax.optimization_barrier((summed, pieces[group]))
         far = jnp.concatenate(pieces[group], axis=1)
         group_state = tuple(part[:, heads] for part in carry_state)
         max_final, denom_final, numerator = absorb(group_state, far, far_source, heads)
-        attn_rows = (numerator / denom_final[:, :, None]).reshape(frames, width * HD)
+        attn_rows = (numerator / denom_final[:, :, None]).reshape(frames, -1)
         partial = jnp.dot(
             attn_rows.astype(jnp.bfloat16),
             gathered_weight[cols],

time: 197 us -> 203 us (1.030)
  waiting for transfers between devices: 100 us -> 110 us
  local copies, waits for them, and re-layouts: 18.5 us -> 15.9 us
    ppermute x10, waiting for transfers between devices: 69.4 us -> 75.6 us  [in_plane(): return lax.ppermute(block, 'ctx', route)]
    ppermute x1, waiting for transfers between devices: 30.3 us -> 33.4 us  [shards(): lax.ppermute(kv_block, 'ctx', [(i, (i + plane_size) % cycle_size) for i i...]
    unnamed x16 -> x14, local copies, waits for them, and re-layouts: 8.93 us -> 7.87 us
  transfers between devices with their start and end apart: 12 -> 12, of which waited for: 4 -> 4; matrix products, arithmetic and copies ran while one was open for 26% -> 27% of each run, Pallas kernels for 0% -> 0%
where the time goes in v3:
time: 203 us; the launch traced here: 202 us
  waiting for transfers between devices  110 us (54%)
  matrix products  35.2 us (17%)
  starting transfers between devices  16.1 us (8%)
  local copies, waits for them, and re-layouts  15.9 us (8%)
  between operations  14 us (7%)
  other arithmetic  11.3 us (6%)
    ppermute x10, waiting for transfers between devices, in_plane(): return lax.ppermute(block, 'ctx', route)  75.6 us
    ppermute x1, waiting for transfers between devices, shards(): lax.ppermute(kv_block, 'ctx', [(i, (i + plane_size) % cycle_size) for i i...  33.4 us
    ppermute x10, starting transfers between devices, in_plane(): return lax.ppermute(block, 'ctx', route)  15.6 us
    dot_general x9, matrix products, attend(): jnp.einsum('qhk,khd->qhd', weights.astype(jnp.bfloat16), value_heads, pre...  14.1 us
    dot_general x2, matrix products, shards(): jnp.dot(attn_rows.astype(jnp.bfloat16), gathered_weight[cols], preferred_...  13.6 us
    unnamed x14, local copies, waits for them, and re-layouts  7.87 us
    dot_general x9, matrix products, attend(): jnp.einsum('qhd,khd->qhk', query_heads, key_heads, preferred_element_type...  7.49 us
    reduce_sum x9, other arithmetic, attend(): denom_new = jnp.sum(weights, axis=2)  7.03 us
  transfers between devices with their start and end apart: 12, of which 4 were waited for; matrix products, arithmetic and copies ran while one was open for 27% of the time, Pallas kernels for 0%

profile of v3, /device:TPU:102, one launch (start us, length us, event | category | flops | bytes accessed | tf_op | source)
XLA Modules:
  0.0 202.3 jit_solution(16125316497197335125)
XLA Ops:
  7.3 1.5 copy.79
  8.8 1.5 copy.80
  10.2 1.5 pad_maximum_fusion
  11.7 1.6 collective-permute-start
  13.3 1.7 collective-permute-start.1
  15.7 1.5 copy.74
  17.2 1.5 copy.149
  18.7 1.6 copy.150
  21.8 1.4 fusion.71
  24.2 36.5 %collective-permute-done = bf16[2,256,2048]{1,2,0:T(8,128)(2,1)} collective-permute-done((bf16[2,256,2048]{1,2,0:T(8,128)(2,1)}, bf16[2,256,2048]{1,2,0:T(8,128)(2,1)}, u32[]{:S(2)}, u32[]{:S(2)}) %collective-permute-start) | collective-permute-done | bytes 2097184 | tf_op jit(solution)/shard_map/ppermute | solution.py:69
  60.7 1.7 fusion.132
  64.3 1.5 bitcast_add_fusion.5
  65.8 1.3 slice.132
  69.6 1.5 bitcast_add_fusion.4
  71.2 3.1 %collective-permute-start.3 = (bf16[2,128,2048]{1,2,0:T(8,128)(2,1)S(1)}, bf16[2,128,2048]{1,2,0:T(8,128)(2,1)S(1)}, u32[]{:S(2)}, u32[]{:S(2)}) collective-permute-start(bf16[2,128,2048]{1,2,0:T(8,128)(2,1)S(1)} %slice.133), channel_id=1, source_target_pairs={{0,3},{1,0},{2,1},{3,2},{4,7},{5,4},{6,5},{7,6},{8,11},{9,8},{10,9... | collective-permute-start | bytes 3145736 | tf_op jit(solution)/shard_map/ppermute | solution.py:69
  74.3 33.4 %collective-permute-done.4 = bf16[2,256,2048]{1,2,0:T(8,128)(2,1)} collective-permute-done((bf16[2,256,2048]{1,2,0:T(8,128)(2,1)}, bf16[2,256,2048]{1,2,0:T(8,128)(2,1)}, u32[]{:S(2)}, u32[]{:S(2)}) %collective-permute-start.4) | collective-permute-done | bytes 2097184 | tf_op jit(solution)/shard_map/ppermute | solution.py:84
  107.7 3.2 %collective-permute-start.6 = (bf16[2,256,2048]{1,2,0:T(8,128)(2,1)}, bf16[2,256,2048]{1,2,0:T(8,128)(2,1)S(1)}, u32[]{:S(2)}, u32[]{:S(2)}) collective-permute-start(bf16[2,256,2048]{1,2,0:T(8,128)(2,1)} %collective-permute-done.4), channel_id=1, source_target_pairs={{0,3},{1,0},{2,1},{3,2},{4,7},{5,4},{6,5},{7,6},{8,11},{9,8},{10,9... | collective-permute-start | bytes 6291464 | tf_op jit(solution)/shard_map/ppermute | solution.py:69
  110.9 1.7 fusion.129
  112.6 0.9 fusion.22
  116.0 1.5 bitcast_add_fusion.3
  118.5 1.5 bitcast_add_fusion.2
  120.0 31.8 %collective-permute-done.5 = bf16[2,256,2048]{1,2,0:T(8,128)(2,1)S(1)} collective-permute-done((bf16[2,256,2048]{1,2,0:T(8,128)(2,1)}, bf16[2,256,2048]{1,2,0:T(8,128)(2,1)S(1)}, u32[]{:S(2)}, u32[]{:S(2)}) %collective-permute-start.5) | collective-permute-done | bytes 2097184 | tf_op jit(solution)/shard_map/ppermute | solution.py:69
  153.9 1.5 bitcast_add_fusion.1
  155.6 3.5 %collective-permute-start.8 = (bf16[2,128,1536]{1,2,0:T(8,128)(2,1)S(1)}, bf16[2,128,1536]{1,2,0:T(8,128)(2,1)S(1)}, u32[]{:S(2)}, u32[]{:S(2)}) collective-permute-start(bf16[2,128,1536]{1,2,0:T(8,128)(2,1)S(1)} %slice.143), channel_id=1, source_target_pairs={{0,3},{1,0},{2,1},{3,2},{4,7},{5,4},{6,5},{7,6},{8,11},{9,8},{10,9... | collective-permute-start | bytes 2359304 | tf_op jit(solution)/shard_map/ppermute | solution.py:69
  161.1 1.5 bitcast_add_fusion
  164.2 2.0 collective-permute-start.9
  166.2 7.2 %collective-permute-done.7 = bf16[2,128,1536]{1,2,0:T(8,128)(2,1)S(1)} collective-permute-done((bf16[2,128,1536]{1,2,0:T(8,128)(2,1)S(1)}, bf16[2,128,1536]{1,2,0:T(8,128)(2,1)S(1)}, u32[]{:S(2)}, u32[]{:S(2)}) %collective-permute-start.7) | collective-permute-done | bytes 786464 | tf_op jit(solution)/shard_map/ppermute | solution.py:69
  175.3 1.9 fusion.77
  177.5 10.0 %fusion = f32[256,4096]{1,0:T(8,128)} fusion(bf16[256,1536]{0,1:T(8,128)(2,1)S(1)} %bitcast.202, bf16[2048,4096]{1,0:T(8,128)(2,1)} %all-gather.2.cloned.1.call-done), kind=kOutput, calls=%fused_computation | convolution fusion | flops 3221225472 | bytes 17563648 | tf_op jit(solution)/shard_map/dot_general | solution.py:120
  188.2 1.6 fusion.98
  189.9 3.6 %fusion.2 = f32[256,4096]{1,0:T(8,128)S(1)} fusion(bf16[256,512]{0,1:T(8,128)(2,1)S(1)} %bitcast.199, bf16[2048,4096]{1,0:T(8,128)(2,1)} %all-gather.2.cloned.1.call-done), kind=kOutput, calls=%fused_computation.2 | convolution fusion | flops 1073741824 | bytes 8650752 | tf_op jit(solution)/shard_map/dot_general | solution.py:120
  193.6 1.8 fusion.42
  (80 shorter events, 20.1 us)
Async XLA Ops:
  6.5 170.9 %all-gather.2.cloned.1.call-start = ((), (), s32[]{:S(2)}) async-start(), calls=%async_computation | async-start | bytes 17825792 | tf_op jit(solution)/shard_map/all_gather | solution.py:57
  7.3 8.3 %copy-start.2 = (s32[1,8]{1,0:T(1,128)S(1)}, s32[1,8]{1,0:T(1,128)}, u32[]{:S(2)}) copy-start(s32[1,8]{1,0:T(1,128)} %param.8) | copy-start | bytes 100
  11.7 49.0 %collective-permute-start = (bf16[2,256,2048]{1,2,0:T(8,128)(2,1)}, bf16[2,256,2048]{1,2,0:T(8,128)(2,1)}, u32[]{:S(2)}, u32[]{:S(2)}) collective-permute-start(bf16[2,256,2048]{1,2,0:T(8,128)(2,1)} %pad_maximum_fusion), channel_id=1, source_target_pairs={{0,1},{1,2},{2,3},{3,0},{4,5},{5,6},{6,7},{7,4},{8,9},{9,10},{10,1... | collective-permute-start | bytes 6291464 | tf_op jit(solution)/shard_map/ppermute | solution.py:69
  13.3 54.3 %collective-permute-start.1 = (bf16[2,256,2048]{1,2,0:T(8,128)(2,1)}, bf16[2,256,2048]{1,2,0:T(8,128)(2,1)S(1)}, u32[]{:S(2)}, u32[]{:S(2)}) collective-permute-start(bf16[2,256,2048]{1,2,0:T(8,128)(2,1)} %pad_maximum_fusion), channel_id=1, source_target_pairs={{0,3},{1,0},{2,1},{3,2},{4,7},{5,4},{6,5},{7,6},{8,11},{9,8},{10,9... | collective-permute-start | bytes 6291464 | tf_op jit(solution)/shard_map/ppermute | solution.py:69
  15.0 92.7 %collective-permute-start.4 = (bf16[2,256,2048]{1,2,0:T(8,128)(2,1)}, bf16[2,256,2048]{1,2,0:T(8,128)(2,1)}, u32[]{:S(2)}, u32[]{:S(2)}) collective-permute-start(bf16[2,256,2048]{1,2,0:T(8,128)(2,1)} %pad_maximum_fusion), channel_id=1, source_target_pairs={{0,4},{1,5},{2,6},{3,7},{4,0},{5,1},{6,2},{7,3},{8,12},{9,13},{10,... | collective-permute-start | bytes 6291464 | tf_op jit(solution)/shard_map/ppermute | solution.py:84
  67.1 46.4 %collective-permute-start.2 = (bf16[2,128,2048]{1,2,0:T(8,128)(2,1)S(1)}, bf16[2,128,2048]{1,2,0:T(8,128)(2,1)S(1)}, u32[]{:S(2)}, u32[]{:S(2)}) collective-permute-start(bf16[2,128,2048]{1,2,0:T(8,128)(2,1)S(1)} %slice.132), channel_id=1, source_target_pairs={{0,1},{1,2},{2,3},{3,0},{4,5},{5,6},{6,7},{7,4},{8,9},{9,10},{10,1... | collective-permute-start | bytes 3145736 | tf_op jit(solution)/shard_map/ppermute | solution.py:69
  71.2 42.5 %collective-permute-start.3 = (bf16[2,128,2048]{1,2,0:T(8,128)(2,1)S(1)}, bf16[2,128,2048]{1,2,0:T(8,128)(2,1)S(1)}, u32[]{:S(2)}, u32[]{:S(2)}) collective-permute-start(bf16[2,128,2048]{1,2,0:T(8,128)(2,1)S(1)} %slice.133), channel_id=1, source_target_pairs={{0,3},{1,0},{2,1},{3,2},{4,7},{5,4},{6,5},{7,6},{8,11},{9,8},{10,9... | collective-permute-start | bytes 3145736 | tf_op jit(solution)/shard_map/ppermute | solution.py:69
  107.7 44.2 %collective-permute-start.5 = (bf16[2,256,2048]{1,2,0:T(8,128)(2,1)}, bf16[2,256,2048]{1,2,0:T(8,128)(2,1)S(1)}, u32[]{:S(2)}, u32[]{:S(2)}) collective-permute-start(bf16[2,256,2048]{1,2,0:T(8,128)(2,1)} %collective-permute-done.4), channel_id=1, source_target_pairs={{0,1},{1,2},{2,3},{3,0},{4,5},{5,6},{6,7},{7,4},{8,9},{9,10},{10,1... | collective-permute-start | bytes 6291464 | tf_op jit(solution)/shard_map/ppermute | solution.py:69
  107.7 47.8 %collective-permute-start.6 = (bf16[2,256,2048]{1,2,0:T(8,128)(2,1)}, bf16[2,256,2048]{1,2,0:T(8,128)(2,1)S(1)}, u32[]{:S(2)}, u32[]{:S(2)}) collective-permute-start(bf16[2,256,2048]{1,2,0:T(8,128)(2,1)} %collective-permute-done.4), channel_id=1, source_target_pairs={{0,3},{1,0},{2,1},{3,2},{4,7},{5,4},{6,5},{7,6},{8,11},{9,8},{10,9... | collective-permute-start | bytes 6291464 | tf_op jit(solution)/shard_map/ppermute | solution.py:69
  155.5 17.9 %collective-permute-start.7 = (bf16[2,128,1536]{1,2,0:T(8,128)(2,1)S(1)}, bf16[2,128,1536]{1,2,0:T(8,128)(2,1)S(1)}, u32[]{:S(2)}, u32[]{:S(2)}) collective-permute-start(bf16[2,128,1536]{1,2,0:T(8,128)(2,1)S(1)} %slice.142), channel_id=1, source_target_pairs={{0,1},{1,2},{2,3},{3,0},{4,5},{5,6},{6,7},{7,4},{8,9},{9,10},{10,1... | collective-permute-start | bytes 2359304 | tf_op jit(solution)/shard_map/ppermute | solution.py:69
  155.6 17.9 %collective-permute-start.8 = (bf16[2,128,1536]{1,2,0:T(8,128)(2,1)S(1)}, bf16[2,128,1536]{1,2,0:T(8,128)(2,1)S(1)}, u32[]{:S(2)}, u32[]{:S(2)}) collective-permute-start(bf16[2,128,1536]{1,2,0:T(8,128)(2,1)S(1)} %slice.143), channel_id=1, source_target_pairs={{0,3},{1,0},{2,1},{3,2},{4,7},{5,4},{6,5},{7,6},{8,11},{9,8},{10,9... | collective-permute-start | bytes 2359304 | tf_op jit(solution)/shard_map/ppermute | solution.py:69
  162.7 12.6 %copy-start.1 = (f32[256,16,128]{2,0,1:T(8,128)}, f32[256,16,128]{2,0,1:T(8,128)S(1)}, u32[]{:S(2)}) copy-start(f32[256,16,128]{2,0,1:T(8,128)S(1)} %bitcast_add_fusion) | copy-start | bytes 6291460
  163.4 24.0 %collective-permute-start.10 = (bf16[2,128,512]{1,2,0:T(8,128)(2,1)}, bf16[2,128,512]{1,2,0:T(8,128)(2,1)S(1)}, u32[]{:S(2)}, u32[]{:S(2)}) collective-permute-start(bf16[2,128,512]{1,2,0:T(8,128)(2,1)} %slice.149), channel_id=1, source_target_pairs={{0,3},{1,0},{2,1},{3,2},{4,7},{5,4},{6,5},{7,6},{8,11},{9,8},{10,9... | collective-permute-start | bytes 786440 | tf_op jit(solution)/shard_map/ppermute | solution.py:69
  164.2 23.3 %collective-permute-start.9 = (bf16[2,128,512]{1,2,0:T(8,128)(2,1)}, bf16[2,128,512]{1,2,0:T(8,128)(2,1)S(1)}, u32[]{:S(2)}, u32[]{:S(2)}) collective-permute-start(bf16[2,128,512]{1,2,0:T(8,128)(2,1)} %slice.148), channel_id=1, source_target_pairs={{0,1},{1,2},{2,3},{3,0},{4,5},{5,6},{6,7},{7,4},{8,9},{9,10},{10,1... | collective-permute-start | bytes 786440 | tf_op jit(solution)/shard_map/ppermute | solution.py:69
  189.9 3.7 %copy-start = (f32[256,4096]{1,0:T(8,128)S(1)}, f32[256,4096]{1,0:T(8,128)}, u32[]{:S(2)}) copy-start(f32[256,4096]{1,0:T(8,128)} %fusion) | copy-start | bytes 12582916
Sparse Core Ops, SparseCore 0:
  9.0 132.1 all-gather.1
